TPU v7x, 128 devices: a whole 4x4x4 slice. The times are simulated.
128 devices in a mesh: dp: 32 (over y, z_lo, x), tensor: 4 (over z_hi, core).
Axes of the slice: x: 4, y: 4, z: 4 (z_hi: 2, z_lo: 2; z = z_hi * 2 + z_lo), core: 2. Of those that a mesh axis runs over, the one named last changes fastest.
Arguments:
- tokens: bfloat16 [32768, 4096], P('dp'), may hold values from -6 to 6
- grad_out: bfloat16 [32768, 2048], P('dp', 'tensor'), may hold values from -12 to 12
- w_query: bfloat16 [4096, 2048], P('dp', 'tensor'), may hold values from -2 to 2
- w_key: bfloat16 [4096, 512], P('dp', 'tensor'), may hold values from -2 to 2
- value_matrix: bfloat16 [4096, 512], P('dp', 'tensor'), may hold values from -0.09375 to 0.09375
Outputs:
- grad_tokens: bfloat16 [32768, 4096], P('dp', 'tensor')
- grad_query: bfloat16 [4096, 2048], P('dp', 'tensor')
- grad_key: bfloat16 [4096, 512], P('dp', 'tensor')
- grad_value: bfloat16 [4096, 512], P('dp', 'tensor')
All inputs are finite; a program needn't handle non-finite values.
Results may differ from a plain program's by a relative error of at most 0.03.
The roundings to bfloat16 on the way count: a program that leaves them out, or rounds other values in their place, can miss the bound.
Values may be sent and summed in bfloat16 or wider, within the bound.
No kernel may reach another device: no remote copies, remote signals or barrier semaphores. Data moves between devices by JAX's collectives and lax.ppermute only.
A program may use at most 192 MiB of HBM per device.

v0:
```python
import jax
import jax.numpy as jnp
from jax import lax
from jax.sharding import PartitionSpec as P

MODEL_WIDTH = 4096
HEAD_SIZE = 128
rope_base = 500000.0


def position_tables(length, head_dim):
    half_dim = head_dim // 2
    positions = jnp.arange(length, dtype=jnp.float32)
    inverse = jnp.power(
        jnp.float32(rope_base), -2.0 * jnp.arange(half_dim, dtype=jnp.float32) / head_dim
    )
    angles = positions[:, None] * inverse[None, :]
    cosine = jnp.concatenate([jnp.cos(angles), jnp.cos(angles)], axis=-1)[:, None, :]
    sine_table = jnp.concatenate([jnp.sin(angles), jnp.sin(angles)], axis=-1)[:, None, :]
    return (cosine, sine_table)


def half_turn(values):
    lower, upper = jnp.split(values, 2, axis=-1)
    return jnp.concatenate([-upper, lower], axis=-1)


def rotate_forward(values, cosine, sine_table):
    return values * cosine + half_turn(values) * sine_table


def rotate_back(grads, cosine, sine_table):
    return grads * cosine - half_turn(grads * sine_table)


def attention_backward(unrotated_query, unrotated_key, projected_value, upstream_flat, kv_heads):
    length = unrotated_query.shape[0]
    heads = unrotated_query.shape[1] // HEAD_SIZE
    group_size = heads // kv_heads
    cosine, sine_table = position_tables(length, HEAD_SIZE)
    query = rotate_forward(
        unrotated_query.reshape(length, heads, HEAD_SIZE), cosine, sine_table
    ).astype(jnp.bfloat16)
    key = rotate_forward(
        unrotated_key.reshape(length, kv_heads, HEAD_SIZE), cosine, sine_table
    ).astype(jnp.bfloat16)
    value = projected_value.reshape(length, kv_heads, HEAD_SIZE).astype(jnp.bfloat16)
    query_grouped = query.reshape(length, kv_heads, group_size, HEAD_SIZE)
    upstream = upstream_flat.reshape(length, kv_heads, group_size, HEAD_SIZE)
    scale = 1.0 / jnp.sqrt(jnp.float32(HEAD_SIZE))
    scores = (
        jnp.einsum("ikgd,jkd->kgij", query_grouped, key, preferred_element_type=jnp.float32) * scale
    )
    positions = jnp.arange(length, dtype=jnp.int32)
    causal = positions[:, None] >= positions[None, :]
    scores = jnp.where(causal, scores, -jnp.inf)
    row_max = jnp.max(scores, axis=-1, keepdims=True)
    weights = jnp.exp(scores - row_max)
    weights = weights / jnp.sum(weights, axis=-1, keepdims=True)
    weights_b = weights.astype(jnp.bfloat16)
    dprob = jnp.einsum("ikgd,jkd->kgij", upstream, value, preferred_element_type=jnp.float32)
    rowdot = jnp.sum(weights * dprob, axis=-1, keepdims=True)
    dscore = (weights * (dprob - rowdot) * scale).astype(jnp.bfloat16)
    dquery = jnp.einsum("kgij,jkd->ikgd", dscore, key, preferred_element_type=jnp.float32).reshape(
        length, heads, HEAD_SIZE
    )
    dkey = jnp.einsum("kgij,ikgd->jkd", dscore, query_grouped, preferred_element_type=jnp.float32)
    dvalue = jnp.einsum("kgij,ikgd->jkd", weights_b, upstream, preferred_element_type=jnp.float32)
    query_gradient = (
        rotate_back(dquery, cosine, sine_table)
        .astype(jnp.bfloat16)
        .reshape(length, heads * HEAD_SIZE)
    )
    key_gradient = (
        rotate_back(dkey, cosine, sine_table)
        .astype(jnp.bfloat16)
        .reshape(length, kv_heads * HEAD_SIZE)
    )
    value_gradient = dvalue.astype(jnp.bfloat16).reshape(length, kv_heads * HEAD_SIZE)
    return (query_gradient, key_gradient, value_gradient)


def contract_cols(grads, weight_rows):
    return lax.dot_general(
        grads, weight_rows, (((1,), (1,)), ((), ())), preferred_element_type=jnp.float32
    )


def body(tokens, grad_out, w_query, w_key, value_matrix):
    query_cols = w_query.shape[1]
    key_value_columns = w_key.shape[1]
    kv_dev = key_value_columns // HEAD_SIZE
    pieces = (
        lax.all_gather(w_query, "dp", axis=0, tiled=True),
        lax.all_gather(w_key, "dp", axis=0, tiled=True),
        lax.all_gather(value_matrix, "dp", axis=0, tiled=True),
    )
    unrotated_query, unrotated_key, projected_value = tuple(
        (jnp.dot(tokens, piece, preferred_element_type=jnp.float32) for piece in pieces)
    )
    query_gradient, key_gradient, value_gradient = attention_backward(
        unrotated_query, unrotated_key, projected_value, grad_out, kv_dev
    )
    combined = jnp.concatenate([query_gradient, key_gradient, value_gradient], axis=1)
    pieces = lax.all_gather((w_query, w_key, value_matrix), "dp", axis=0, tiled=True)
    partial_sum = (
        contract_cols(query_gradient, pieces[0])
        + contract_cols(key_gradient, pieces[1])
        + contract_cols(value_gradient, pieces[2])
    )
    summed_all = lax.psum(partial_sum.astype(jnp.bfloat16), "tensor").astype(jnp.float32)
    share_width = MODEL_WIDTH // lax.axis_size("tensor")
    grad_tokens = lax.dynamic_slice_in_dim(
        summed_all, lax.axis_index("tensor") * share_width, share_width, 1
    )
    grads_all = lax.psum_scatter(
        lax.dot_general(
            tokens, combined, (((0,), (0,)), ((), ())), preferred_element_type=jnp.float32
        ).astype(jnp.bfloat16),
        "dp",
        scatter_dimension=0,
        tiled=True,
    ).astype(jnp.float32)
    grad_query = grads_all[:, :query_cols].astype(jnp.bfloat16)
    grad_key = grads_all[:, query_cols : query_cols + key_value_columns].astype(jnp.bfloat16)
    grad_value = grads_all[:, query_cols + key_value_columns :].astype(jnp.bfloat16)
    return (grad_tokens.astype(jnp.bfloat16), grad_query, grad_key, grad_value)


def solution(mesh):
    in_specs = (
        P("dp", None),
        P("dp", "tensor"),
        P("dp", "tensor"),
        P("dp", "tensor"),
        P("dp", "tensor"),
    )
    out_specs = (P("dp", "tensor"), P("dp", "tensor"), P("dp", "tensor"), P("dp", "tensor"))
    return jax.shard_map(body, mesh=mesh, in_specs=in_specs, out_specs=out_specs, check_vma=False)
```

profile of v0, /device:TPU:0, one launch (start us, length us, event | category | flops | bytes accessed | tf_op | source)
XLA Modules:
  0.0 889.6 jit_solution(15293957988102845399)
XLA Ops:
  7.2 0.0 all-gather.4.cloned.1.call-start
  7.2 0.7 all-gather.4.cloned.1.call-update
  7.9 0.0 all-gather.6.cloned.1.call-start
  7.9 0.7 all-gather.6.cloned.1.call-update
  8.6 0.0 all-gather.8.cloned.1.call-start
  8.7 0.7 all-gather.8.cloned.1.call-update
  9.4 0.0 all-reduce.2.cloned.1.call-start
  9.4 0.3 iota_compare_fusion
  9.8 1.0 fusion.38
  10.8 0.0 copy-start.10
  10.8 2.4 copy.40
  13.1 149.9 %all-gather.4.cloned.1.call-done = bf16[4096,128]{1,0:T(8,128)(2,1)} async-done(((bf16[128,128]{1,0:T(8,128)(2,1)}), bf16[4096,128]{1,0:T(8,128)(2,1)}) %all-gather.4.cloned.1.call-update) | async-done | bytes 1048592 | tf_op jit(solution)/shard_map/all_gather | solution.py:95
  163.1 6.5 fusion.43
  169.6 1.2 pad_maximum_fusion.1
  170.8 151.1 %all-gather.6.cloned.1.call-done = bf16[4096,512]{1,0:T(8,128)(2,1)} async-done(((bf16[128,512]{1,0:T(8,128)(2,1)}), bf16[4096,512]{1,0:T(8,128)(2,1)}) %all-gather.6.cloned.1.call-update) | async-done | bytes 4194320 | tf_op jit(solution)/shard_map/all_gather | solution.py:94
  321.9 8.3 fusion.44
  330.2 0.2 slice_negate_fusion.1
  330.4 0.2 maximum_multiply_fusion
  330.6 0.0 copy-start.1
  330.6 0.6 copy-done.3
  331.2 0.6 fusion.14
  331.8 0.1 copy-done.1
  331.9 3.1 fusion.6
  335.1 3.6 fusion.5
  338.7 2.3 copy-done
  341.0 6.0 fusion.25
  347.0 127.4 %all-gather.8.cloned.1.call-done = bf16[4096,128]{1,0:T(8,128)(2,1)} async-done(((bf16[128,128]{1,0:T(8,128)(2,1)}), bf16[4096,128]{1,0:T(8,128)(2,1)}) %all-gather.8.cloned.1.call-update) | async-done | bytes 1048592 | tf_op jit(solution)/shard_map/all_gather | solution.py:96
  474.4 18.2 %fusion = (f32[4,1024]{1,0:T(4,128)S(1)}, f32[1024,1024,4]{1,0,2:T(8,128)}) fusion(f32[4,1024]{1,0:T(4,128)S(1)} %fusion.5, f32[4,1024]{1,0:T(4,128)S(1)} %get-tuple-element.27, f32[1024,1024,4]{1,0,2:T(8,128)} %copy-done, pred[1024,1024]{0,1:T(8,128)(4,1)S(1)} %iota_compare_fusion, bf16[1024,4,128]{0,2,1:T(8,128)(2,1)} %bitcast.132, ...), kind=kOutput, calls=%fused_computation.3 | convolution fusion | flops 2172776448 | bytes 45137920 | tf_op jit(solution)/shard_map/ikgd,jkd->kgij/dot_general | solution.py:61
  492.7 13.4 %fusion.7 = bf16[4,1024,1024]{1,2,0:T(8,128)(2,1)S(1)} fusion(f32[1024,1024,4]{1,0,2:T(8,128)} %get-tuple-element.30, f32[4,1024]{1,0:T(4,128)S(1)} %get-tuple-element.29, f32[4,1024]{1,0:T(4,128)S(1)} %fusion.5, f32[4,1024]{1,0:T(4,128)S(1)} %get-tuple-element.27, f32[1024,1024,4]{1,0,2:T(8,128)} %copy-done, pred[1024,1024]{0,1:T(8,128)(4,1)S(1)} %iota_compare_fusion), kind=kLoop, calls=%fused_computation.12 | loop fusion | flops 33554432 | bytes 43040768 | tf_op jit(solution)/shard_map/reshape.19
  506.1 3.0 bitcast_multiply_fusion.4
  509.1 1.4 bitcast_multiply_fusion.3
  510.5 0.3 slice_negate_fusion
  510.8 0.2 pad_maximum_fusion
  511.0 0.6 fusion.16
  511.7 0.1 fusion.34
  511.8 8.1 fusion.46
  519.9 8.1 fusion.45
  528.0 15.3 %add_convert_fusion = bf16[1024,4096]{1,0:T(8,128)(2,1)} fusion(f32[1024,4096]{1,0:T(8,128)} %fusion.45, f32[1024,4096]{1,0:T(8,128)} %fusion.46, bf16[1024,128]{0,1:T(8,128)(2,1)S(1)} %copy-done.14, bf16[4096,128]{1,0:T(8,128)(2,1)S(1)} %copy-done.13), kind=kOutput, calls=%fused_computation.7 | convolution fusion | flops 1086324736 | bytes 43253760 | tf_op jit(solution)/shard_map/dot_general | solution.py:84
  543.4 0.0 all-reduce.2.cloned.1.call-update
  543.4 0.0 reduce-scatter.4.cloned.1.call-start
  543.4 13.3 %fusion.11 = bf16[4096,768]{0,1:T(8,128)(2,1)} fusion(bf16[1024,4096]{1,0:T(8,128)(2,1)} %param.5, bf16[1024,128]{0,1:T(8,128)(2,1)S(1)} %copy-done.14, bf16[1024,128]{0,1:T(8,128)(2,1)S(1)} %fusion.34, bf16[1024,512]{0,1:T(8,128)(2,1)S(1)} %fusion.16), kind=kOutput, calls=%fused_computation.17 | convolution fusion | flops 6450315264 | bytes 16252928 | tf_op jit(solution)/shard_map/dot_general | solution.py:117
  556.7 8.5 copy.35
  565.2 0.0 reduce-scatter.4.cloned.1.call-update
  565.2 138.8 %all-reduce.2.cloned.1.call-done = bf16[1024,4096]{1,0:T(8,128)(2,1)} async-done(((bf16[1024,4096]{1,0:T(8,128)(2,1)}), bf16[1024,4096]{1,0:T(8,128)(2,1)}) %all-reduce.2.cloned.1.call-update) | async-done | bytes 8388624 | tf_op jit(solution)/shard_map/psum | solution.py:111
  704.0 3.1 convert_convert_fusion
  707.1 173.1 %reduce-scatter.4.cloned.1.call-done = bf16[128,768]{1,0:T(8,128)(2,1)} async-done(((bf16[4096,768]{1,0:T(8,128)(2,1)}), bf16[128,768]{1,0:T(8,128)(2,1)}) %reduce-scatter.4.cloned.1.call-update) | async-done | bytes 196624
  880.1 1.6 slice.15
  881.7 1.4 fusion.42
  (30 shorter events, 0.1 us)
Async XLA Ops:
  7.2 155.9 %all-gather.4.cloned.1.call-start = ((), (), s32[]{:S(2)}) async-start(), calls=%async_computation.1 | async-start | bytes 1081344 | tf_op jit(solution)/shard_map/all_gather | solution.py:95
  7.9 314.0 %all-gather.6.cloned.1.call-start = ((), (), s32[]{:S(2)}) async-start(), calls=%async_computation.2 | async-start | bytes 4325376 | tf_op jit(solution)/shard_map/all_gather | solution.py:94
  8.6 465.8 %all-gather.8.cloned.1.call-start = ((), (), s32[]{:S(2)}) async-start(), calls=%async_computation.3 | async-start | bytes 1081344 | tf_op jit(solution)/shard_map/all_gather | solution.py:96
  9.4 694.6 %all-reduce.2.cloned.1.call-start = ((), (), s32[]{:S(2)}) async-start(), calls=%async_computation.4 | async-start | bytes 16777216 | tf_op jit(solution)/shard_map/psum | solution.py:111
  10.8 158.9 %copy-start.10 = (f32[1024,64]{0,1:T(8,128)}, f32[1024,64]{0,1:T(8,128)S(1)}, u32[]{:S(2)}) copy-start(f32[1024,64]{0,1:T(8,128)S(1)} %get-tuple-element.25) | copy-start | bytes 786436
  321.9 8.5 copy-start.5
  330.2 1.0 copy-start.3
  330.2 1.7 copy-start.8
  330.6 1.3 copy-start.1
  335.0 5.9 copy-start
  335.1 5.9 copy-start.12
  492.6 13.4 %copy-start.2 = (f32[1024,4,128]{0,2,1:T(8,128)S(1)}, f32[1024,4,128]{0,2,1:T(8,128)}, u32[]{:S(2)}) copy-start(f32[1024,4,128]{0,2,1:T(8,128)} %copy-done.1) | copy-start | bytes 6291460
  492.7 13.4 %copy-start.4 = (f32[1024,128]{0,1:T(8,128)S(1)}, f32[1024,128]{0,1:T(8,128)}, u32[]{:S(2)}) copy-start(f32[1024,128]{0,1:T(8,128)} %get-tuple-element.20) | copy-start | bytes 1572868
  506.1 3.0 copy-start.6
  506.1 3.0 copy-start.9
  510.5 1.2 copy-start.11
  510.5 1.3 copy-start.7
  511.8 8.1 copy-start.15
  519.9 8.1 copy-start.13
  519.9 8.1 copy-start.14
  543.4 336.8 %reduce-scatter.4.cloned.1.call-start = ((), (), s32[]{:S(2)}) async-start(), calls=%async_computation.5 | async-start | bytes 6488064
Sparse Core Ops, SparseCore 0:
  9.6 153.3 all-gather.3
  164.7 157.1 all-gather.5
  323.5 150.8 all-gather.7
  543.5 160.4 all-reduce.1
  706.3 173.8 reduce-scatter.3
where the time goes:
time: 890 us
  waiting for transfers between devices  742 us (83%)
  matrix products  91.3 us (10%)
  other arithmetic  24.8 us (3%)
  local copies, waits for them, and re-layouts  16.8 us (2%)
  between operations  14.1 us (2%)
    unnamed x6, waiting for transfers between devices  175 us
    all_gather x1, waiting for transfers between devices, body(): lax.all_gather(w_query, 'dp', axis=0, tiled=True)  151 us
    all_gather x1, waiting for transfers between devices, body(): lax.all_gather(w_key, 'dp', axis=0, tiled=True)  150 us
    psum x1, waiting for transfers between devices, body(): lax.psum(partial_sum.astype(jnp.bfloat16), 'tensor').astype(jnp.float32)  139 us
    all_gather x1, waiting for transfers between devices, body(): lax.all_gather(value_matrix, 'dp', axis=0, tiled=True)  127 us
    dot_general x3, matrix products, contract_cols(): lax.dot_general(grads, weight_rows, (((1,), (1,)), ((), ())), preferred_e...  31.5 us
    dot_general x1, matrix products, attention_backward(): jnp.einsum('ikgd,jkd->kgij', upstream, value, preferred_element_type=jnp....  18.2 us
  transfers between devices with their start and end apart: 5, of which 5 were waited for; matrix products, arithmetic and copies ran while one was open for 7% of the time, Pallas kernels for 0%

commit v1 on v0

--- a/solution.py
+++ b/solution.py
@@ -1,3 +1,4 @@
+import functools
 import jax
 import jax.numpy as jnp
 from jax import lax
@@ -6,6 +7,16 @@
 MODEL_WIDTH = 4096
 HEAD_SIZE = 128
 rope_base = 500000.0
+
+
+def assign_inputs_on(local_block, axis_name):
+    f_next = lax.all_to_all(
+        jnp.stack([local_block] * lax.axis_size(axis_name), axis=0), axis_name, 0, 0
+    )
+    return jnp.concatenate(f_next, 0)
+
+
+wrap_ranges_by_axis = functools.partial(assign_inputs_on, axis_name="dp")
 
 
 def position_tables(length, head_dim):
@@ -93,7 +104,7 @@
     pieces = (
         lax.all_gather(w_query, "dp", axis=0, tiled=True),
         lax.all_gather(w_key, "dp", axis=0, tiled=True),
-        lax.all_gather(value_matrix, "dp", axis=0, tiled=True),
+        wrap_ranges_by_axis(value_matrix),
     )
     unrotated_query, unrotated_key, projected_value = tuple(
         (jnp.dot(tokens, piece, preferred_element_type=jnp.float32) for piece in pieces)

time: 890 us -> 839 us (0.943)
  waiting for transfers between devices: 742 us -> 676 us
    all_gather x1, waiting for transfers between devices: 127 us -> 69.6 us  [body(): lax.all_gather((w_query, w_key, value_matrix), 'dp', axis=0, tiled=True)]
    all_gather x1, waiting for transfers between devices: 150 us -> 140 us  [body(): lax.all_gather(w_key, 'dp', axis=0, tiled=True)]
  transfers between devices with their start and end apart: 5 -> 6, of which waited for: 5 -> 5; matrix products, arithmetic and copies ran while one was open for 7% -> 14% of each run, Pallas kernels for 0% -> 0%
where the time goes in v1:
time: 839 us; the launch traced here: 838 us
  waiting for transfers between devices  676 us (81%)
  matrix products  92.4 us (11%)
  other arithmetic  24.6 us (3%)
  local copies, waits for them, and re-layouts  22.5 us (3%)
  between operations  14.1 us (2%)
  starting transfers between devices  9.08 us (1%)
    unnamed x6, waiting for transfers between devices  175 us
    all_gather x1, waiting for transfers between devices, body(): lax.all_gather(w_query, 'dp', axis=0, tiled=True)  152 us
    all_gather x1, waiting for transfers between devices, body(): lax.all_gather(w_key, 'dp', axis=0, tiled=True)  140 us
    psum x1, waiting for transfers between devices, body(): lax.psum(partial_sum.astype(jnp.bfloat16), 'tensor').astype(jnp.float32)  139 us
    all_gather x1, waiting for transfers between devices, body(): lax.all_gather((w_query, w_key, value_matrix), 'dp', axis=0, tiled=True)  69.6 us
    dot_general x3, matrix products, contract_cols(): lax.dot_general(grads, weight_rows, (((1,), (1,)), ((), ())), preferred_e...  33.5 us
    dot_general x1, matrix products, attention_backward(): jnp.einsum('ikgd,jkd->kgij', upstream, value, preferred_element_type=jnp....  18.4 us
  transfers between devices with their start and end apart: 6, of which 5 were waited for; matrix products, arithmetic and copies ran while one was open for 14% of the time, Pallas kernels for 0%

profile of v1, /device:TPU:0, one launch (start us, length us, event | category | flops | bytes accessed | tf_op | source)
XLA Modules:
  0.0 838.3 jit_solution(16931385308182861579)
XLA Ops:
  7.2 0.0 all-gather.4.cloned.1.call-start
  7.2 0.7 all-gather.4.cloned.1.call-update
  7.9 0.0 all-gather.6.cloned.1.call-start
  7.9 0.7 all-gather.6.cloned.1.call-update
  8.6 2.0 stack.2
  10.6 8.9 %all-to-all-start = ((bf16[32,128,128]{2,1,0:T(8,128)(2,1)}), bf16[32,128,128]{2,1,0:T(8,128)(2,1)}, u32[]{:S(2)}, u32[]{:S(2)}) async-start(bf16[32,128,128]{2,1,0:T(8,128)(2,1)} %stack.2), calls=%async_computation | async-start | bytes 2097152 | tf_op jit(solution)/shard_map/all_to_all | solution.py:13
  19.5 0.0 all-gather.8.cloned.1.call-start
  19.6 0.7 all-gather.8.cloned.1.call-update
  20.2 0.0 all-reduce.2.cloned.1.call-start
  20.3 0.3 iota_compare_fusion
  20.6 1.0 fusion.38
  21.6 2.4 copy.40
  24.0 139.9 %all-gather.4.cloned.1.call-done = bf16[4096,128]{1,0:T(8,128)(2,1)} async-done(((bf16[128,128]{1,0:T(8,128)(2,1)}), bf16[4096,128]{1,0:T(8,128)(2,1)}) %all-gather.4.cloned.1.call-update) | async-done | bytes 1048592 | tf_op jit(solution)/shard_map/all_gather | solution.py:106
  163.9 6.5 fusion.43
  170.5 1.2 pad_maximum_fusion.1
  171.7 152.1 %all-gather.6.cloned.1.call-done = bf16[4096,512]{1,0:T(8,128)(2,1)} async-done(((bf16[128,512]{1,0:T(8,128)(2,1)}), bf16[4096,512]{1,0:T(8,128)(2,1)}) %all-gather.6.cloned.1.call-update) | async-done | bytes 4194320 | tf_op jit(solution)/shard_map/all_gather | solution.py:105
  323.8 8.3 fusion.44
  332.1 0.2 slice_negate_fusion.1
  332.2 0.2 maximum_multiply_fusion
  332.5 0.6 copy-done.3
  333.1 0.6 fusion.14
  333.7 0.1 copy-done.1
  333.8 3.1 fusion.6
  336.9 5.7 copy-done
  342.6 3.6 fusion.5
  346.3 18.4 %fusion = (f32[4,1024]{1,0:T(4,128)S(1)}, f32[1024,1024,4]{1,0,2:T(8,128)}) fusion(f32[4,1024]{1,0:T(4,128)S(1)} %fusion.5, f32[4,1024]{1,0:T(4,128)S(1)} %get-tuple-element.27, f32[1024,1024,4]{1,0,2:T(8,128)} %copy-done, pred[1024,1024]{0,1:T(8,128)(4,1)S(1)} %iota_compare_fusion, bf16[1024,4,128]{0,2,1:T(8,128)(2,1)} %bitcast.135, ...), kind=kOutput, calls=%fused_computation.3 | convolution fusion | flops 2172776448 | bytes 45137920 | tf_op jit(solution)/shard_map/ikgd,jkd->kgij/dot_general | solution.py:72
  364.7 13.2 %fusion.7 = bf16[4,1024,1024]{1,2,0:T(8,128)(2,1)S(1)} fusion(f32[1024,1024,4]{1,0,2:T(8,128)} %get-tuple-element.30, f32[4,1024]{1,0:T(4,128)S(1)} %get-tuple-element.29, f32[4,1024]{1,0:T(4,128)S(1)} %fusion.5, f32[4,1024]{1,0:T(4,128)S(1)} %get-tuple-element.27, f32[1024,1024,4]{1,0,2:T(8,128)} %copy-done, pred[1024,1024]{0,1:T(8,128)(4,1)S(1)} %iota_compare_fusion), kind=kLoop, calls=%fused_computation.12 | loop fusion | flops 33554432 | bytes 43040768 | tf_op jit(solution)/shard_map/reshape.21
  378.0 3.0 bitcast_multiply_fusion.4
  381.0 1.4 bitcast_multiply_fusion.3
  382.4 0.3 slice_negate_fusion
  382.7 0.2 pad_maximum_fusion
  382.9 0.6 fusion.16
  383.6 0.1 fusion.34
  383.8 9.4 %fusion.46 = f32[1024,4096]{1,0:T(8,128)} fusion(bf16[1024,128]{0,1:T(8,128)(2,1)S(1)} %fusion.34, bf16[4096,128]{1,0:T(8,128)(2,1)S(1)} %copy-done.7), kind=kOutput, calls=%fused_computation.70 | convolution fusion | flops 1073741824 | bytes 18087936 | tf_op jit(solution)/shard_map/dot_general | solution.py:95
  393.2 8.4 fusion.45
  401.6 5.2 fusion.25
  406.8 69.6 %all-gather.8.cloned.1.call-done = bf16[4096,128]{1,0:T(8,128)(2,1)} async-done(((bf16[128,128]{1,0:T(8,128)(2,1)}), bf16[4096,128]{1,0:T(8,128)(2,1)}) %all-gather.8.cloned.1.call-update) | async-done | bytes 1048592 | tf_op jit(solution)/shard_map/all_gather | solution.py:116
  476.4 15.7 %add_convert_fusion = bf16[1024,4096]{1,0:T(8,128)(2,1)} fusion(f32[1024,4096]{1,0:T(8,128)} %fusion.45, f32[1024,4096]{1,0:T(8,128)} %fusion.46, bf16[1024,128]{0,1:T(8,128)(2,1)S(1)} %fusion.25, bf16[4096,128]{1,0:T(8,128)(2,1)} %all-gather.8.cloned.1.call-done), kind=kOutput, calls=%fused_computation.7 | convolution fusion | flops 1086324736 | bytes 43253760 | tf_op jit(solution)/shard_map/dot_general | solution.py:95
  492.1 0.0 all-reduce.2.cloned.1.call-update
  492.1 0.0 reduce-scatter.4.cloned.1.call-start
  492.1 13.1 %fusion.11 = bf16[4096,768]{0,1:T(8,128)(2,1)} fusion(bf16[1024,4096]{1,0:T(8,128)(2,1)} %param.5, bf16[1024,128]{0,1:T(8,128)(2,1)S(1)} %fusion.25, bf16[1024,128]{0,1:T(8,128)(2,1)S(1)} %fusion.34, bf16[1024,512]{0,1:T(8,128)(2,1)S(1)} %fusion.16), kind=kOutput, calls=%fused_computation.17 | convolution fusion | flops 6450315264 | bytes 16252928 | tf_op jit(solution)/shard_map/dot_general | solution.py:128
  505.2 8.6 %copy.35 = bf16[4096,768]{1,0:T(8,128)(2,1)} copy(bf16[4096,768]{0,1:T(8,128)(2,1)} %fusion.11) | data formatting | bytes 12582912
  513.8 0.0 reduce-scatter.4.cloned.1.call-update
  513.9 138.7 %all-reduce.2.cloned.1.call-done = bf16[1024,4096]{1,0:T(8,128)(2,1)} async-done(((bf16[1024,4096]{1,0:T(8,128)(2,1)}), bf16[1024,4096]{1,0:T(8,128)(2,1)}) %all-reduce.2.cloned.1.call-update) | async-done | bytes 8388624 | tf_op jit(solution)/shard_map/psum | solution.py:122
  652.6 3.1 convert_convert_fusion
  655.7 173.1 %reduce-scatter.4.cloned.1.call-done = bf16[128,768]{1,0:T(8,128)(2,1)} async-done(((bf16[4096,768]{1,0:T(8,128)(2,1)}), bf16[128,768]{1,0:T(8,128)(2,1)}) %reduce-scatter.4.cloned.1.call-update) | async-done | bytes 196624
  828.8 1.6 slice.15
  830.3 1.4 fusion.42
  (38 shorter events, 0.2 us)
Async XLA Ops:
  7.2 156.8 %all-gather.4.cloned.1.call-start = ((), (), s32[]{:S(2)}) async-start(), calls=%async_computation.2 | async-start | bytes 1081344 | tf_op jit(solution)/shard_map/all_gather | solution.py:106
  7.9 315.9 %all-gather.6.cloned.1.call-start = ((), (), s32[]{:S(2)}) async-start(), calls=%async_computation.3 | async-start | bytes 4325376 | tf_op jit(solution)/shard_map/all_gather | solution.py:105
  10.6 335.7 %all-to-all-start = ((bf16[32,128,128]{2,1,0:T(8,128)(2,1)}), bf16[32,128,128]{2,1,0:T(8,128)(2,1)}, u32[]{:S(2)}, u32[]{:S(2)}) async-start(bf16[32,128,128]{2,1,0:T(8,128)(2,1)} %stack.2), calls=%async_computation | async-start | bytes 2097152 | tf_op jit(solution)/shard_map/all_to_all | solution.py:13
  19.5 456.9 %all-gather.8.cloned.1.call-start = ((), (), s32[]{:S(2)}) async-start(), calls=%async_computation.4 | async-start | bytes 1081344 | tf_op jit(solution)/shard_map/all_gather | solution.py:116
  20.2 632.4 %all-reduce.2.cloned.1.call-start = ((), (), s32[]{:S(2)}) async-start(), calls=%async_computation.5 | async-start | bytes 16777216 | tf_op jit(solution)/shard_map/psum | solution.py:122
  21.6 148.9 %copy-start.10 = (f32[1024,64]{0,1:T(8,128)}, f32[1024,64]{0,1:T(8,128)S(1)}, u32[]{:S(2)}) copy-start(f32[1024,64]{0,1:T(8,128)S(1)} %get-tuple-element.25) | copy-start | bytes 786436
  323.8 8.5 %copy-start.5 = (f32[1024,128]{0,1:T(8,128)S(1)}, f32[1024,128]{0,1:T(8,128)}, u32[]{:S(2)}) copy-start(f32[1024,128]{0,1:T(8,128)} %get-tuple-element.22) | copy-start | bytes 1572868
  332.1 1.0 copy-start.3
  332.1 1.7 copy-start.8
  332.5 1.3 copy-start.1
  336.9 5.8 copy-start
  364.7 13.2 %copy-start.2 = (f32[1024,4,128]{0,2,1:T(8,128)S(1)}, f32[1024,4,128]{0,2,1:T(8,128)}, u32[]{:S(2)}) copy-start(f32[1024,4,128]{0,2,1:T(8,128)} %copy-done.1) | copy-start | bytes 6291460
  364.7 13.2 %copy-start.4 = (f32[1024,128]{0,1:T(8,128)S(1)}, f32[1024,128]{0,1:T(8,128)}, u32[]{:S(2)}) copy-start(f32[1024,128]{0,1:T(8,128)} %get-tuple-element.20) | copy-start | bytes 1572868
  378.0 3.0 copy-start.6
  378.0 3.0 copy-start.9
  382.4 1.2 copy-start.11
  382.4 1.4 copy-start.7
  383.7 9.5 %copy-start.13 = (bf16[4096,512]{1,0:T(8,128)(2,1)S(1)}, bf16[4096,512]{1,0:T(8,128)(2,1)}, u32[]{:S(2)}) copy-start(bf16[4096,512]{1,0:T(8,128)(2,1)} %all-gather.6.cloned.1.call-done) | copy-start | bytes 12582916
  383.7 17.9 %slice-start = ((s8[16777216]{0:T(1024)(128)(4,1)}), s8[4194304]{0:T(1024)(128)(4,1)S(1)}, s32[]{:S(2)}) async-start(s8[16777216]{0:T(1024)(128)(4,1)} %bitcast.129), calls=%async_computation.7 | async-start | bytes 8388608
  383.7 17.8 %slice-start.1 = ((s8[16777216]{0:T(1024)(128)(4,1)}), s8[4194304]{0:T(1024)(128)(4,1)S(1)}, s32[]{:S(2)}) async-start(s8[16777216]{0:T(1024)(128)(4,1)} %bitcast.129), calls=%async_computation.8 | async-start | bytes 8388608
  393.2 8.4 %slice-start.2 = ((s8[16777216]{0:T(1024)(128)(4,1)}), s8[4194304]{0:T(1024)(128)(4,1)S(1)}, s32[]{:S(2)}) async-start(s8[16777216]{0:T(1024)(128)(4,1)} %bitcast.129), calls=%async_computation.9 | async-start | bytes 8388608
  393.2 8.4 %slice-start.3 = ((s8[16777216]{0:T(1024)(128)(4,1)}), s8[4194304]{0:T(1024)(128)(4,1)S(1)}, s32[]{:S(2)}) async-start(s8[16777216]{0:T(1024)(128)(4,1)} %bitcast.129), calls=%async_computation.10 | async-start | bytes 8388608
  393.2 8.4 %copy-start.12 = (bf16[1024,512]{0,1:T(8,128)(2,1)S(1)}, bf16[1024,512]{0,1:T(8,128)(2,1)}, u32[]{:S(2)}) copy-start(bf16[1024,512]{0,1:T(8,128)(2,1)} %copy.40) | copy-start | bytes 3145732
  492.1 336.7 %reduce-scatter.4.cloned.1.call-start = ((), (), s32[]{:S(2)}) async-start(), calls=%async_computation.6 | async-start | bytes 6488064
Sparse Core Ops, SparseCore 0:
  9.6 154.2 all-gather.3
  165.6 158.1 all-gather.5
  325.4 150.9 all-gather.7
  492.2 160.3 all-reduce.1
  654.9 173.8 reduce-scatter.3
